TPU v7x, 32 devices: a whole 2x2x4 slice. The times are simulated.
32 devices in a mesh: uv: 8 (over z, y), tm: 4 (over x, core).
Axes of the slice: x: 2, y: 2, z: 4, core: 2. Of those that a mesh axis runs over, the one named last changes fastest.
Arguments:
- visibility: bfloat16 [4, 1024, 2048], P('tm', 'uv'), may hold values from -1536 to 1536
- anchor: int32 [4, 1024], P('tm', 'uv'), may hold values from 0 to 80
- offset: int32 [4, 1024], P('tm', 'uv'), may hold values from 0 to 63
- slot_rows: int32 [4, 8, 8, 32], P('tm', 'uv'), may hold values from 0 to 127, as said below
- counts: int32 [4, 8, 8], P('tm', 'uv'), may hold values from 0 to 32, as said below
Outputs:
- delay: float32 [2048, 2048], P(('uv', 'tm'))
Inputs may be any that keep to these rules, and one draw needn't show every extreme that they name: For every g and s the first counts[g, s, d] entries of slot_rows[g, s, d] over all d name each of the 128 rows of device s exactly once; entries at slots k >= counts[g, s, d] are arbitrary rows and are not used. counts[g, s, :] sums to 128; in each time group one tile receives 32 rows from every device and another tile none; the other tiles come in pairs whose counts from one device sum to 32.
All inputs are finite; a program needn't handle non-finite values.
Results may differ from a plain program's by a relative error of at most 0.0047.
Values may be sent and summed in bfloat16 or wider, within the bound.
No kernel may reach another device: no remote copies, remote signals or barrier semaphores. Data moves between devices by JAX's collectives and lax.ppermute only.
A program may use at most 64 MiB of HBM per device.

v0:
```python
import math
import jax
import jax.numpy as jnp
from jax import lax
from jax.sharding import PartitionSpec as P

NCH = 1024
ROWS_DEV = 128
TS = 16
KTAPS = 8
OSAMP = 8


def kernel_taps(offsets):
    tap_index = jnp.arange(KTAPS, dtype=jnp.float32)
    sub_shift = (offsets.astype(jnp.float32) + 0.5) / OSAMP
    distance = tap_index[None, :] - (KTAPS / 2 - 1.0) - sub_shift[:, None]
    return jnp.exp(-distance * distance / (2.0 * 1.2 * 1.2))


def tap_matrix(cell_ids, anchors, offsets):
    span = TS - KTAPS + 1
    anchor_y = anchors // span
    anchor_x = anchors % span
    taps_y = kernel_taps(offsets // OSAMP)
    taps_x = kernel_taps(offsets % OSAMP)
    cell_y = cell_ids // TS
    cell_x = cell_ids % TS
    along_y = jnp.zeros((cell_ids.shape[0], anchors.shape[0]), jnp.float32)
    along_x = jnp.zeros((cell_ids.shape[0], anchors.shape[0]), jnp.float32)
    for step in range(KTAPS):
        along_y = along_y + jnp.where(
            cell_y[:, None] == anchor_y[None, :] + step, taps_y[None, :, step], 0.0
        )
        along_x = along_x + jnp.where(
            cell_x[:, None] == anchor_x[None, :] + step, taps_x[None, :, step], 0.0
        )
    return (along_y * along_x).astype(jnp.bfloat16)


def delay_table():
    freq = jnp.arange(NCH, dtype=jnp.int32)
    phase = freq[:, None] * freq[None, :] % NCH
    angle = 2.0 * math.pi / NCH * phase.astype(jnp.float32)
    cosine = jnp.cos(angle)
    sine = jnp.sin(angle)
    window_arg = 2.0 * math.pi * freq.astype(jnp.float32) / (NCH - 1)
    taper = (
        0.35875
        - 0.48829 * jnp.cos(window_arg)
        + 0.14128 * jnp.cos(2.0 * window_arg)
        - 0.01168 * jnp.cos(3.0 * window_arg)
    )
    tap_cos = taper[:, None] * cosine
    tap_sin = taper[:, None] * sine
    upper = jnp.concatenate([tap_cos, -tap_sin], axis=1)
    lower = jnp.concatenate([tap_sin, tap_cos], axis=1)
    return jnp.concatenate([upper, lower], axis=0).astype(jnp.bfloat16)


def per_device(visibility, anchor, offset, slot_rows, counts):
    time_groups = lax.axis_size("tm")
    cell_share = TS * TS // time_groups
    vis_rows = visibility[0]
    row_width = vis_rows.shape[1]
    slot_table = slot_rows[0, 0]
    tile_count, slot_depth = slot_table.shape
    is_live = (jnp.arange(slot_depth, dtype=jnp.int32)[None, :] < counts[0, 0][:, None]).reshape(-1)
    flat_index = slot_table.reshape(-1)
    outgoing = jnp.where(
        is_live[:, None], jnp.take(vis_rows, flat_index, axis=0), jnp.zeros((), vis_rows.dtype)
    )
    outgoing = outgoing.reshape(tile_count, slot_depth, row_width)
    out_anchor = jnp.take(anchor[0], flat_index).reshape(tile_count, slot_depth)
    out_offset = jnp.take(offset[0], flat_index).reshape(tile_count, slot_depth)
    arrived, arr_anchor, arr_offset = (
        lax.all_to_all(outgoing, "uv", split_axis=0, concat_axis=0, tiled=True),
        lax.all_to_all(out_anchor, "uv", split_axis=0, concat_axis=0, tiled=True),
        lax.all_to_all(out_offset, "uv", split_axis=0, concat_axis=0, tiled=True),
    )
    my_start = lax.axis_index("tm") * cell_share
    all_cells = jnp.arange(TS * TS, dtype=jnp.int32)
    weights = tap_matrix(all_cells, arr_anchor.reshape(-1), arr_offset.reshape(-1))
    flat_vis = arrived.reshape(-1, row_width)
    full_sum = lax.psum(jnp.dot(weights, flat_vis, preferred_element_type=jnp.float32), "tm")
    summed = lax.dynamic_slice_in_dim(full_sum, my_start, cell_share, 0)
    grid = summed.astype(jnp.bfloat16)
    transform = delay_table()
    out_scale = 4.0 / math.sqrt(NCH * time_groups * ROWS_DEV)
    return jnp.dot(grid, transform, preferred_element_type=jnp.float32) * out_scale


def solution(mesh):
    in_specs = (
        P("tm", "uv", None),
        P("tm", "uv"),
        P("tm", "uv"),
        P("tm", "uv", None, None),
        P("tm", "uv", None),
    )
    out_specs = P(("uv", "tm"), None)
    return jax.shard_map(
        per_device, mesh=mesh, in_specs=in_specs, out_specs=out_specs, check_vma=False
    )
```

profile of v0, /device:TPU:0, one launch (start us, length us, event | category | flops | bytes accessed | tf_op | source)
XLA Modules:
  0.0 105.8 jit_solution(13739666395043265725)
XLA Ops:
  0.0 0.0 copy-start
  0.0 0.0 copy-start.2
  0.0 0.0 copy-start.3
  0.0 0.8 reshape_squeeze.7
  0.9 1.9 %gather_fusion.2 = s32[256]{0:T(256)S(1)} fusion(s32[128]{0:T(128)} %bitcast.33, s32[1024]{0:T(1024)S(1)} %pad_clamp_fusion.1), kind=kCustom, calls=%fused_computation.1.clone | custom fusion | bytes 3072 | tf_op jit(solution)/shard_map/jit(_take)/gather | solution.py:75
  2.7 1.9 %gather_fusion.1 = s32[256]{0:T(256)S(1)} fusion(s32[128]{0:T(128)} %bitcast.34, s32[1024]{0:T(1024)S(1)} %pad_clamp_fusion.1), kind=kCustom, calls=%fused_computation.clone | custom fusion | bytes 3072 | tf_op jit(solution)/shard_map/jit(_take)/gather | solution.py:74
  4.7 0.7 all_to_all.17
  5.3 7.3 %all-to-all-start.1 = ((s32[8,1,32]{2,1,0:T(1,128)}), s32[8,1,32]{2,1,0:T(1,128)S(1)}, u32[]{:S(2)}, u32[]{:S(2)}) async-start(s32[8,1,32]{2,1,0:T(1,128)} %all_to_all.17), calls=%async_computation.1 | async-start | bytes 8192 | tf_op jit(solution)/shard_map/all_to_all | solution.py:79
  12.6 0.0 copy-done.2
  12.6 0.1 reshape_squeeze.9
  12.7 0.1 multiply_subtract_fusion
  12.8 0.0 copy-done.3
  12.8 0.1 iota_compare_fusion
  12.9 0.0 copy-done
  12.9 1.4 %gather_fusion = bf16[256,2048]{1,0:T(8,128)(2,1)S(1)} fusion(bf16[128,2048]{1,0:T(8,128)(2,1)S(1)} %bitcast.32, s32[1024]{0:T(1024)S(1)} %pad_clamp_fusion), kind=kCustom, calls=%fused_computation.2 | custom fusion | bytes 2098176 | tf_op jit(solution)/shard_map/jit(_take)/gather | solution.py:71
  14.2 1.2 %select_select_fusion = bf16[8,32,2048]{2,1,0:T(8,128)(2,1)} fusion(bf16[8,32,2048]{2,1,0:T(8,128)(2,1)S(1)} %bitcast.35, pred[8,32]{1,0:T(8,128)(4,1)S(1)} %get-tuple-element.60, pred[8,32]{1,0:T(8,128)(4,1)S(1)} %get-tuple-element.59), kind=kLoop, calls=%fused_computation.25 | loop fusion | flops 1048576 | bytes 2097664 | tf_op jit(solution)/shard_map/jit(_where)/select_n | solution.py:70
  15.4 0.7 all_to_all.15
  16.1 2.9 %all-to-all-done.1 = s32[8,1,32]{2,1,0:T(1,128)S(1)} async-done(((s32[8,1,32]{2,1,0:T(1,128)}), s32[8,1,32]{2,1,0:T(1,128)S(1)}, u32[]{:S(2)}, u32[]{:S(2)}) %all-to-all-start.1) | async-done | bytes 1056 | tf_op jit(solution)/shard_map/all_to_all | solution.py:79
  19.0 3.2 %all-to-all-start = ((s32[8,1,32]{2,1,0:T(1,128)}), s32[8,1,32]{2,1,0:T(1,128)S(1)}, u32[]{:S(2)}, u32[]{:S(2)}) async-start(s32[8,1,32]{2,1,0:T(1,128)} %all_to_all.15), calls=%async_computation | async-start | bytes 8192 | tf_op jit(solution)/shard_map/all_to_all | solution.py:78
  22.3 6.4 %all-to-all-done = s32[8,1,32]{2,1,0:T(1,128)S(1)} async-done(((s32[8,1,32]{2,1,0:T(1,128)}), s32[8,1,32]{2,1,0:T(1,128)S(1)}, u32[]{:S(2)}, u32[]{:S(2)}) %all-to-all-start) | async-done | bytes 1056 | tf_op jit(solution)/shard_map/all_to_all | solution.py:78
  28.7 3.6 %all-to-all-start.2 = ((bf16[8,32,2048]{2,1,0:T(8,128)(2,1)}), bf16[8,32,2048]{2,1,0:T(8,128)(2,1)S(1)}, u32[]{:S(2)}, u32[]{:S(2)}) async-start(bf16[8,32,2048]{2,1,0:T(8,128)(2,1)} %select_select_fusion), calls=%async_computation.2 | async-start | bytes 2097152 | tf_op jit(solution)/shard_map/all_to_all | solution.py:77
  32.2 19.1 %negate_convert_fusion = (bf16[1024,1024]{1,0:T(8,128)(2,1)}, bf16[1024,1024]{1,0:T(8,128)(2,1)}, bf16[1024,1024]{1,0:T(8,128)(2,1)}) fusion(f32[1024]{0:T(1024)S(1)} %multiply_subtract_fusion), kind=kLoop, calls=%fused_computation.17 | loop fusion | flops 20971520 | bytes 6295552 | tf_op jit(solution)/shard_map/convert.5
  51.3 0.5 broadcast.585
  51.8 0.7 reduce.13
  52.5 0.1 reshape.340
  52.6 0.1 ne.248
  52.7 0.1 div.91
  52.8 0.1 rem.188
  52.9 0.1 fusion.55
  53.0 3.3 %all-to-all-done.2 = bf16[8,32,2048]{2,1,0:T(8,128)(2,1)S(1)} async-done(((bf16[8,32,2048]{2,1,0:T(8,128)(2,1)}), bf16[8,32,2048]{2,1,0:T(8,128)(2,1)S(1)}, u32[]{:S(2)}, u32[]{:S(2)}) %all-to-all-start.2) | async-done | bytes 1048608 | tf_op jit(solution)/shard_map/all_to_all | solution.py:77
  56.3 0.0 copy-start.1
  56.3 1.0 copy-done.1
  57.3 2.1 %fusion.18 = f32[256,2048]{1,0:T(8,128)S(1)} fusion(bf16[256,2048]{1,0:T(8,128)(2,1)} %bitcast.36, f32[256]{0:T(256)S(1)} %bitcast.52, s32[256]{0:T(256)S(1)} %get-tuple-element.46, f32[256]{0:T(256)S(1)} %bitcast.51, s32[256]{0:T(256)S(1)} %get-tuple-element.42, f32[256]{0:T(256)S(1)} %bitcast.50, s32[256]{0:T(256)S(1)} %get-tuple-element.43, ...), kind=kOutput, calls=%fused_computation.28 | convolution fusion | flops 271581184 | bytes 3180544 | tf_op jit(solution)/shard_map/dot_general | solution.py:85
  59.4 40.5 %all-reduce.1 = bf16[256,2048]{1,0:T(8,128)(2,1)} all-reduce(f32[256,2048]{1,0:T(8,128)S(1)} %fusion.18), channel_id=1, replica_groups=mesh['uv'=8,'tm'=4] {'tm'}, use_global_device_ids=true, to_apply=%region_0.0 | all-reduce | flops 524288 | bytes 3145728 | tf_op jit(solution)/shard_map/psum | solution.py:85
  99.9 5.9 %fusion.15 = f32[64,2048]{1,0:T(8,128)} fusion(bf16[1024,1024]{1,0:T(8,128)(2,1)} %get-tuple-element.30, bf16[1024,1024]{1,0:T(8,128)(2,1)} %get-tuple-element.29, bf16[1024,1024]{1,0:T(8,128)(2,1)} %get-tuple-element.28, bf16[256,2048]{1,0:T(8,128)(2,1)} %all-reduce.1, s32[]{:T(128)S(6)} %select_n.242), kind=kOutput, calls=%fused_computation.24 | convolution fusion | flops 570556416 | bytes 7077892 | tf_op jit(solution)/shard_map/dot_general | solution.py:90
  (13 shorter events, 0.2 us)
Async XLA Ops:
  0.0 12.9 %copy-start = (bf16[1,128,2048]{2,1,0:T(8,128)(2,1)S(1)}, bf16[1,128,2048]{2,1,0:T(8,128)(2,1)}, u32[]{:S(2)}) copy-start(bf16[1,128,2048]{2,1,0:T(8,128)(2,1)} %param.7) | copy-start | bytes 1572868
  0.0 12.6 %copy-start.2 = (s32[1,1,8,32]{3,2,1,0:T(8,128)S(1)}, s32[1,1,8,32]{3,2,1,0:T(8,128)}, u32[]{:S(2)}) copy-start(s32[1,1,8,32]{3,2,1,0:T(8,128)} %param.10) | copy-start | bytes 3076
  0.0 12.8 %copy-start.3 = (s32[1,1,8]{2,1,0:T(1,128)S(1)}, s32[1,1,8]{2,1,0:T(1,128)}, u32[]{:S(2)}) copy-start(s32[1,1,8]{2,1,0:T(1,128)} %param.11) | copy-start | bytes 100
  5.3 13.7 %all-to-all-start.1 = ((s32[8,1,32]{2,1,0:T(1,128)}), s32[8,1,32]{2,1,0:T(1,128)S(1)}, u32[]{:S(2)}, u32[]{:S(2)}) async-start(s32[8,1,32]{2,1,0:T(1,128)} %all_to_all.17), calls=%async_computation.1 | async-start | bytes 8192 | tf_op jit(solution)/shard_map/all_to_all | solution.py:79
  19.0 9.7 %all-to-all-start = ((s32[8,1,32]{2,1,0:T(1,128)}), s32[8,1,32]{2,1,0:T(1,128)S(1)}, u32[]{:S(2)}, u32[]{:S(2)}) async-start(s32[8,1,32]{2,1,0:T(1,128)} %all_to_all.15), calls=%async_computation | async-start | bytes 8192 | tf_op jit(solution)/shard_map/all_to_all | solution.py:78
  28.7 27.6 %all-to-all-start.2 = ((bf16[8,32,2048]{2,1,0:T(8,128)(2,1)}), bf16[8,32,2048]{2,1,0:T(8,128)(2,1)S(1)}, u32[]{:S(2)}, u32[]{:S(2)}) async-start(bf16[8,32,2048]{2,1,0:T(8,128)(2,1)} %select_select_fusion), calls=%async_computation.2 | async-start | bytes 2097152 | tf_op jit(solution)/shard_map/all_to_all | solution.py:77
  56.3 1.0 copy-start.1
where the time goes:
time: 106 us
  blocking collectives  40.5 us (38%)
  other arithmetic  21.3 us (20%)
  starting transfers between devices  14.1 us (13%)
  waiting for transfers between devices  12.6 us (12%)
  local copies, waits for them, and re-layouts  9.27 us (9%)
  matrix products  7.99 us (8%)
    psum x1, blocking collectives, per_device(): lax.psum(jnp.dot(weights, flat_vis, preferred_element_type=jnp.float32),...  40.5 us
    another operation x1, other arithmetic  19.1 us
    all_to_all x1, starting transfers between devices, per_device(): lax.all_to_all(out_offset, 'uv', split_axis=0, concat_axis=0, tiled=True)  7.28 us
    all_to_all x1, waiting for transfers between devices, per_device(): lax.all_to_all(out_anchor, 'uv', split_axis=0, concat_axis=0, tiled=True)  6.38 us
    dot_general x1, matrix products, per_device(): jnp.dot(grid, transform, preferred_element_type=jnp.float32) * out_scale  5.92 us
    all_to_all x1, starting transfers between devices, per_device(): lax.all_to_all(outgoing, 'uv', split_axis=0, concat_axis=0, tiled=True)  3.56 us
    all_to_all x1, waiting for transfers between devices, per_device(): lax.all_to_all(outgoing, 'uv', split_axis=0, concat_axis=0, tiled=True)  3.3 us
    all_to_all x1, starting transfers between devices, per_device(): lax.all_to_all(out_anchor, 'uv', split_axis=0, concat_axis=0, tiled=True)  3.25 us
  transfers between devices with their start and end apart: 3, of which 3 were waited for; matrix products, arithmetic and copies ran while one was open for 22% of the time, Pallas kernels for 0%

commit v1 on v0

--- a/solution.py
+++ b/solution.py
@@ -82,7 +82,9 @@
     all_cells = jnp.arange(TS * TS, dtype=jnp.int32)
     weights = tap_matrix(all_cells, arr_anchor.reshape(-1), arr_offset.reshape(-1))
     flat_vis = arrived.reshape(-1, row_width)
-    full_sum = lax.psum(jnp.dot(weights, flat_vis, preferred_element_type=jnp.float32), "tm")
+    full_sum = jnp.sum(
+        lax.all_gather(jnp.dot(weights, flat_vis, preferred_element_type=jnp.float32), "tm"), axis=0
+    )
     summed = lax.dynamic_slice_in_dim(full_sum, my_start, cell_share, 0)
     grid = summed.astype(jnp.bfloat16)
     transform = delay_table()

time: 106 us -> 149 us (1.41)
  waiting for transfers between devices: 12.6 us -> 69 us
  blocking collectives: 40.5 us -> 0 us
  between operations: 0.12 us -> 13.5 us
  matrix products: 7.99 us -> 15.8 us
  other arithmetic: 21.3 us -> 26.8 us
    psum x1 -> x0, blocking collectives: 40.5 us -> none  [per_device(): lax.psum(jnp.dot(weights, flat_vis, preferred_element_type=jnp.float32),...]
    all_gather x0 -> x1, waiting for transfers between devices: none -> 38.9 us  [per_device(): lax.all_gather(jnp.dot(weights, flat_vis, preferred_element_type=jnp.floa...]
    all_to_all x1, waiting for transfers between devices: 3.3 us -> 22.1 us  [per_device(): lax.all_to_all(outgoing, 'uv', split_axis=0, concat_axis=0, tiled=True)]
    dot_general x1, matrix products: 5.92 us -> 13.6 us  [per_device(): jnp.dot(grid, transform, preferred_element_type=jnp.float32) * out_scale]
    reduce_sum x0 -> x1, other arithmetic: none -> 5.53 us  [per_device(): jnp.sum(lax.all_gather(jnp.dot(weights, flat_vis, preferred_element_type=...]
    all_to_all x1, starting transfers between devices: 3.25 us -> 7.28 us  [per_device(): lax.all_to_all(out_anchor, 'uv', split_axis=0, concat_axis=0, tiled=True)]
    all_to_all x1, starting transfers between devices: 7.28 us -> 3.31 us  [per_device(): lax.all_to_all(out_offset, 'uv', split_axis=0, concat_axis=0, tiled=True)]
    all_to_all x1, waiting for transfers between devices: 6.38 us -> 2.86 us  [per_device(): lax.all_to_all(out_anchor, 'uv', split_axis=0, concat_axis=0, tiled=True)]
  transfers between devices with their start and end apart: 3 -> 4, of which waited for: 3 -> 4; matrix products, arithmetic and copies ran while one was open for 22% -> 16% of each run, Pallas kernels for 0% -> 0%
where the time goes in v1:
time: 149 us; the launch traced here: 148 us
  waiting for transfers between devices  69 us (46%)
  other arithmetic  26.8 us (18%)
  matrix products  15.8 us (11%)
  starting transfers between devices  14.4 us (10%)
  between operations  13.5 us (9%)
  local copies, waits for them, and re-layouts  8.95 us (6%)
    all_gather x1, waiting for transfers between devices, per_device(): lax.all_gather(jnp.dot(weights, flat_vis, preferred_element_type=jnp.floa...  38.9 us
    all_to_all x1, waiting for transfers between devices, per_device(): lax.all_to_all(outgoing, 'uv', split_axis=0, concat_axis=0, tiled=True)  22.1 us
    another operation x1, other arithmetic  18.4 us
    dot_general x1, matrix products, per_device(): jnp.dot(grid, transform, preferred_element_type=jnp.float32) * out_scale  13.6 us
    all_to_all x1, starting transfers between devices, per_device(): lax.all_to_all(out_anchor, 'uv', split_axis=0, concat_axis=0, tiled=True)  7.28 us
    reduce_sum x1, other arithmetic, per_device(): jnp.sum(lax.all_gather(jnp.dot(weights, flat_vis, preferred_element_type=...  5.53 us
    all_to_all x1, waiting for transfers between devices, per_device(): lax.all_to_all(out_offset, 'uv', split_axis=0, concat_axis=0, tiled=True)  5.15 us
    all_to_all x1, starting transfers between devices, per_device(): lax.all_to_all(outgoing, 'uv', split_axis=0, concat_axis=0, tiled=True)  3.56 us
  transfers between devices with their start and end apart: 4, of which 4 were waited for; matrix products, arithmetic and copies ran while one was open for 16% of the time, Pallas kernels for 0%

profile of v1, /device:TPU:0, one launch (start us, length us, event | category | flops | bytes accessed | tf_op | source)
XLA Modules:
  0.0 148.4 jit_solution(8674068299946302563)
XLA Ops:
  6.5 0.0 copy-start
  6.5 0.8 reshape_squeeze.7
  7.4 1.9 %gather_fusion.1 = s32[256]{0:T(256)S(1)} fusion(s32[128]{0:T(128)} %bitcast.34, s32[1024]{0:T(1024)S(1)} %pad_clamp_fusion.1), kind=kCustom, calls=%fused_computation.clone | custom fusion | bytes 3072 | tf_op jit(solution)/shard_map/jit(_take)/gather | solution.py:74
  9.3 1.9 %gather_fusion.2 = s32[256]{0:T(256)S(1)} fusion(s32[128]{0:T(128)} %bitcast.35, s32[1024]{0:T(1024)S(1)} %pad_clamp_fusion.1), kind=kCustom, calls=%fused_computation.1.clone | custom fusion | bytes 3072 | tf_op jit(solution)/shard_map/jit(_take)/gather | solution.py:75
  11.2 0.7 all_to_all.15
  11.9 7.3 %all-to-all-start = ((s32[8,1,32]{2,1,0:T(1,128)}), s32[8,1,32]{2,1,0:T(1,128)S(1)}, u32[]{:S(2)}, u32[]{:S(2)}) async-start(s32[8,1,32]{2,1,0:T(1,128)} %all_to_all.15), calls=%async_computation | async-start | bytes 8192 | tf_op jit(solution)/shard_map/all_to_all | solution.py:78
  19.1 0.8 reshape_squeeze.9
  19.9 0.8 iota_compare_fusion
  20.7 0.7 all_to_all.17
  21.4 0.0 copy-done
  21.4 1.4 gather_fusion
  22.7 2.9 %all-to-all-done = s32[8,1,32]{2,1,0:T(1,128)S(1)} async-done(((s32[8,1,32]{2,1,0:T(1,128)}), s32[8,1,32]{2,1,0:T(1,128)S(1)}, u32[]{:S(2)}, u32[]{:S(2)}) %all-to-all-start) | async-done | bytes 1056 | tf_op jit(solution)/shard_map/all_to_all | solution.py:78
  25.6 3.3 %all-to-all-start.1 = ((s32[8,1,32]{2,1,0:T(1,128)}), s32[8,1,32]{2,1,0:T(1,128)S(1)}, u32[]{:S(2)}, u32[]{:S(2)}) async-start(s32[8,1,32]{2,1,0:T(1,128)} %all_to_all.17), calls=%async_computation.1 | async-start | bytes 8192 | tf_op jit(solution)/shard_map/all_to_all | solution.py:79
  28.9 1.2 select_select_fusion
  30.1 5.1 %all-to-all-done.1 = s32[8,1,32]{2,1,0:T(1,128)S(1)} async-done(((s32[8,1,32]{2,1,0:T(1,128)}), s32[8,1,32]{2,1,0:T(1,128)S(1)}, u32[]{:S(2)}, u32[]{:S(2)}) %all-to-all-start.1) | async-done | bytes 1056 | tf_op jit(solution)/shard_map/all_to_all | solution.py:79
  35.3 3.6 %all-to-all-start.2 = ((bf16[8,32,2048]{2,1,0:T(8,128)(2,1)}), bf16[8,32,2048]{2,1,0:T(8,128)(2,1)S(1)}, u32[]{:S(2)}, u32[]{:S(2)}) async-start(bf16[8,32,2048]{2,1,0:T(8,128)(2,1)} %select_select_fusion), calls=%async_computation.2 | async-start | bytes 2097152 | tf_op jit(solution)/shard_map/all_to_all | solution.py:77
  38.8 0.2 all-gather.3.cloned.1.call-start
  39.1 0.1 div.91
  39.2 0.1 rem.188
  39.3 0.1 ne.248
  39.4 0.5 broadcast.585
  39.9 0.7 reduce.13
  40.6 0.1 reshape.340
  40.7 0.1 fusion.55
  40.8 22.1 %all-to-all-done.2 = bf16[8,32,2048]{2,1,0:T(8,128)(2,1)S(1)} async-done(((bf16[8,32,2048]{2,1,0:T(8,128)(2,1)}), bf16[8,32,2048]{2,1,0:T(8,128)(2,1)S(1)}, u32[]{:S(2)}, u32[]{:S(2)}) %all-to-all-start.2) | async-done | bytes 1048608 | tf_op jit(solution)/shard_map/all_to_all | solution.py:77
  62.9 2.2 %fusion.18 = f32[256,2048]{1,0:T(8,128)} fusion(bf16[256,2048]{1,0:T(8,128)(2,1)S(1)} %bitcast.38, f32[256]{0:T(256)S(1)} %bitcast.54, s32[256]{0:T(256)S(1)} %get-tuple-element.46, f32[256]{0:T(256)S(1)} %bitcast.53, s32[256]{0:T(256)S(1)} %get-tuple-element.42, f32[256]{0:T(256)S(1)} %bitcast.52, s32[256]{0:T(256)S(1)} %get-tuple-element.43, ...), kind=kOutput, calls=%fused_computation.28 | convolution fusion | flops 271581184 | bytes 3180544 | tf_op jit(solution)/shard_map/dot_general | solution.py:86
  65.1 0.0 all-gather.3.cloned.1.call-update
  65.1 0.1 multiply_subtract_fusion
  65.2 18.4 %negate_convert_fusion = (bf16[1024,1024]{1,0:T(8,128)(2,1)S(1)}, bf16[1024,1024]{1,0:T(8,128)(2,1)}, bf16[1024,1024]{1,0:T(8,128)(2,1)}) fusion(f32[1024]{0:T(1024)S(1)} %multiply_subtract_fusion), kind=kLoop, calls=%fused_computation.17 | loop fusion | flops 20971520 | bytes 6295552 | tf_op jit(solution)/shard_map/convert.5
  83.6 38.9 %all-gather.3.cloned.1.call-done = f32[1024,2048]{1,0:T(8,128)} async-done(((f32[256,2048]{1,0:T(8,128)}), f32[1024,2048]{1,0:T(8,128)}) %all-gather.3.cloned.1.call-update) | async-done | bytes 8388624 | tf_op jit(solution)/shard_map/all_gather | solution.py:86
  122.4 5.5 %reduce_sum.9 = bf16[256,2048]{1,0:T(8,128)(2,1)} reduce(f32[4,256,2048]{2,1,0:T(8,128)} %bitcast.36, f32[]{:T(128)} %constant.137.clone.1), dimensions={0}, to_apply=%region_0.0 | reduce | flops 1572864 | bytes 9437188 | tf_op jit(solution)/shard_map/reduce_sum | solution.py:85
  128.0 13.6 %fusion.15 = f32[64,2048]{1,0:T(8,128)} fusion(bf16[1024,1024]{1,0:T(8,128)(2,1)} %get-tuple-element.30, bf16[1024,1024]{1,0:T(8,128)(2,1)} %get-tuple-element.29, bf16[1024,1024]{1,0:T(8,128)(2,1)S(1)} %get-tuple-element.28, bf16[256,2048]{1,0:T(8,128)(2,1)} %reduce_sum.9, s32[]{:T(128)S(6)} %select_n.242), kind=kOutput, calls=%fused_computation.24 | convolution fusion | flops 570556416 | bytes 7077892 | tf_op jit(solution)/shard_map/dot_general | solution.py:92
  (13 shorter events, 0.2 us)
Async XLA Ops:
  6.5 14.8 %copy-start = (bf16[1,128,2048]{2,1,0:T(8,128)(2,1)S(1)}, bf16[1,128,2048]{2,1,0:T(8,128)(2,1)}, u32[]{:S(2)}) copy-start(bf16[1,128,2048]{2,1,0:T(8,128)(2,1)} %param.7) | copy-start | bytes 1572868
  11.9 13.7 %all-to-all-start = ((s32[8,1,32]{2,1,0:T(1,128)}), s32[8,1,32]{2,1,0:T(1,128)S(1)}, u32[]{:S(2)}, u32[]{:S(2)}) async-start(s32[8,1,32]{2,1,0:T(1,128)} %all_to_all.15), calls=%async_computation | async-start | bytes 8192 | tf_op jit(solution)/shard_map/all_to_all | solution.py:78
  25.6 9.6 %all-to-all-start.1 = ((s32[8,1,32]{2,1,0:T(1,128)}), s32[8,1,32]{2,1,0:T(1,128)S(1)}, u32[]{:S(2)}, u32[]{:S(2)}) async-start(s32[8,1,32]{2,1,0:T(1,128)} %all_to_all.17), calls=%async_computation.1 | async-start | bytes 8192 | tf_op jit(solution)/shard_map/all_to_all | solution.py:79
  35.3 27.6 %all-to-all-start.2 = ((bf16[8,32,2048]{2,1,0:T(8,128)(2,1)}), bf16[8,32,2048]{2,1,0:T(8,128)(2,1)S(1)}, u32[]{:S(2)}, u32[]{:S(2)}) async-start(bf16[8,32,2048]{2,1,0:T(8,128)(2,1)} %select_select_fusion), calls=%async_computation.2 | async-start | bytes 2097152 | tf_op jit(solution)/shard_map/all_to_all | solution.py:77
  38.8 83.6 %all-gather.3.cloned.1.call-start = ((), (), s32[]{:S(2)}) async-start(), calls=%async_computation.3 | async-start | bytes 10485760 | tf_op jit(solution)/shard_map/all_gather | solution.py:86
Sparse Core Ops, SparseCore 0:
  65.2 57.1 all-gather.2
